TPU v7x, 32 devices: a whole 2x2x4 slice. The times are simulated.
32 devices in a mesh: seq: 4 (over y, x), tp: 8 (over z, core).
Axes of the slice: x: 2, y: 2, z: 4, core: 2. Of those that a mesh axis runs over, the one named last changes fastest.
Arguments:
- streams: bfloat16 [3, 4096, 1024], P(None, 'tp', 'seq'), may hold values from -6 to 6
- feat_weight: float32 [3, 4096, 7], P(None, 'tp'), may hold values from -2 to 2
- long_filter: float32 [4096, 128], P('tp'), may hold values from -0.5 to 0.5
- skip_gain: float32 [4096], P('tp'), may hold values from -1 to 1
- out_weight: bfloat16 [4096, 4096], P('tp', 'seq'), may hold values from -0.125 to 0.125
- out_grad: bfloat16 [4096, 1024], P('tp', 'seq'), may hold values from -6 to 6
Outputs:
- mixed: bfloat16 [4096, 1024], P('tp', 'seq')
- stream_grad: bfloat16 [3, 4096, 1024], P(None, 'tp', 'seq')
- weight_grad: bfloat16 [4096, 4096], P('tp', 'seq')
All inputs are finite; a program needn't handle non-finite values.
Results may differ from a plain program's by a relative error of at most 0.009.
Values may be sent and summed in bfloat16 or wider, within the bound.
No kernel may reach another device: no remote copies, remote signals or barrier semaphores. Data moves between devices by JAX's collectives and lax.ppermute only.
A program may use at most 64 MiB of HBM per device.

v0:
```python
import math
import jax
import jax.numpy as jnp
from jax import lax
from jax.sharding import PartitionSpec as P


def extended(block, sides, width):
    for axis, dim in sides:
        count = lax.axis_size(axis)
        forward = [(i, i + 1) for i in range(count - 1)]
        backward = [(target, source) for source, target in forward]
        low = lax.ppermute(
            lax.slice_in_dim(block, block.shape[dim] - width, None, axis=dim), axis, forward
        )
        high = lax.ppermute(lax.slice_in_dim(block, 0, width, axis=dim), axis, backward)
        block = jnp.concatenate([low, block, high], axis=dim)
    return block


def from_behind(block, axis, distance):
    devices = range(lax.axis_size(axis))
    route = [(i - distance, i) for i in devices if i - distance in devices]
    return lax.ppermute(block, axis, route)


def correlate(signal, taps):
    return lax.conv_general_dilated(
        signal[None],
        taps[:, None, :],
        (1,),
        "VALID",
        dimension_numbers=("NCH", "OIH", "NCH"),
        feature_group_count=signal.shape[0],
        precision=lax.Precision.HIGHEST,
    )[0]


def rows_of_slab(out_grad, n_seq, n_tp):
    rows, length = out_grad.shape
    piece = rows // n_seq
    split = out_grad.reshape(n_seq, piece, length)
    mine = lax.all_to_all(split, "seq", 0, 0)
    mine = jnp.transpose(mine, (1, 0, 2)).reshape(piece, n_seq * length)
    route = []
    for a in range(n_seq):
        for b in range(n_tp):
            flat = n_seq * b + a
            route.append((a * n_tp + b, flat // n_tp * n_tp + flat % n_tp))
    moved = lax.ppermute(mine, ("seq", "tp"), route)
    return lax.all_gather(moved, "tp", axis=0, tiled=True)


def shards(streams, feat_weight, long_filter, skip_gain, out_weight, out_grad):
    channels = streams.shape[1]
    length = streams.shape[2]
    taps_long = long_filter.shape[1]
    taps_short = feat_weight.shape[2]
    n_seq = lax.axis_size("seq")
    n_tp = lax.axis_size("tp")
    reach = taps_long + taps_short - 2
    slab_grad = rows_of_slab(out_grad, n_seq, n_tp)
    slab_width = slab_grad.shape[0]
    partial_grad = jnp.dot(out_weight, slab_grad, preferred_element_type=jnp.float32)
    gated_grad = lax.psum_scatter(partial_grad, "seq", scatter_dimension=1, tiled=True)
    widened = extended(streams, (("seq", 2),), reach).astype(jnp.float32)
    short_taps = feat_weight.reshape(3 * channels, taps_short)
    feats = correlate(
        widened.reshape(3 * channels, length + 2 * reach), short_taps[:, ::-1]
    ).reshape(3, channels, -1)
    query_feat, key_feat, value_feat = (feats[0], feats[1], feats[2])
    product = key_feat * value_feat
    convolved = correlate(product, long_filter[:, ::-1])
    summed = convolved + skip_gain[:, None] * product[:, taps_long - 1 :]
    query_tail = query_feat[:, taps_long - 1 :]
    gated = (query_tail[:, :length] * summed[:, :length]).astype(jnp.bfloat16)
    gated_all = lax.all_gather(gated, "seq", axis=1, tiled=True)
    partial_out = lax.dot_general(
        out_weight, gated_all, (((0,), (0,)), ((), ())), preferred_element_type=jnp.float32
    )
    group = n_tp // n_seq
    out_rows = slab_width // group
    partial_out = (
        partial_out.reshape(group, out_rows, n_seq, length)
        .transpose(0, 2, 1, 3)
        .reshape(n_tp * out_rows, length)
    )
    output_sum = lax.psum_scatter(partial_out, "tp", scatter_dimension=0, tiled=True)
    route = []
    for s in range(n_seq):
        for p in range(n_tp):
            route.append((s * n_tp + p, p % n_seq * n_tp + group * s + p // n_seq))
    mixed = lax.ppermute(output_sum.astype(jnp.bfloat16), ("seq", "tp"), route)
    scale = 1.0 / math.sqrt(length * n_seq)
    terms = lax.dot_general(
        gated_all.reshape(channels, n_seq, length),
        slab_grad.reshape(slab_width, n_seq, length),
        (((2,), (2,)), ((1,), (1,))),
        preferred_element_type=jnp.float32,
    )
    terms = lax.reduce_precision(terms * scale, exponent_bits=8, mantissa_bits=7)
    weight_grad = jnp.sum(terms, axis=0).astype(jnp.bfloat16)
    next_grad = from_behind(gated_grad[:, :reach].astype(jnp.bfloat16), "seq", -1).astype(
        jnp.float32
    )
    grad_ext = jnp.concatenate([gated_grad, next_grad], axis=1)
    conv_grad = grad_ext * query_tail
    keep = length + taps_short - 1
    prod_grad = correlate(conv_grad, long_filter) + skip_gain[:, None] * conv_grad[:, :keep]
    query_grad = grad_ext[:, :keep] * summed[:, :keep]
    key_grad = prod_grad * value_feat[:, taps_long - 1 : taps_long - 1 + keep]
    value_grad = prod_grad * key_feat[:, taps_long - 1 : taps_long - 1 + keep]
    feat_grad = jnp.stack([query_grad, key_grad, value_grad]).reshape(3 * channels, keep)
    stream_grad = correlate(feat_grad, short_taps).reshape(3, channels, length).astype(jnp.bfloat16)
    return (mixed, stream_grad, weight_grad)


def solution(mesh):
    return jax.shard_map(
        shards,
        mesh=mesh,
        in_specs=(
            P(None, "tp", "seq"),
            P(None, "tp", None),
            P("tp", None),
            P("tp"),
            P("tp", "seq"),
            P("tp", "seq"),
        ),
        out_specs=(P("tp", "seq"), P(None, "tp", "seq"), P("tp", "seq")),
        check_vma=False,
    )
```

profile of v0, /device:TPU:4, one launch (start us, length us, event | category | flops | bytes accessed | tf_op | source)
XLA Modules:
  0.0 241.9 jit_solution(13884115816914673931)
XLA Ops:
  7.2 4.4 %all-to-all-start = ((bf16[4,128,256]{2,1,0:T(8,128)(2,1)}), bf16[4,128,256]{2,1,0:T(8,128)(2,1)S(1)}, u32[]{:S(2)}, u32[]{:S(2)}) async-start(bf16[4,128,256]{2,1,0:T(8,128)(2,1)} %bitcast.78), calls=%async_computation.1 | async-start | bytes 524288 | tf_op jit(solution)/shard_map/all_to_all | solution.py:43
  11.5 1.8 fusion.35
  13.4 1.0 copy.89
  14.4 3.4 %collective-permute-start = (bf16[3,512,133]{1,2,0:T(8,128)(2,1)}, bf16[3,512,133]{1,2,0:T(8,128)(2,1)S(1)}, u32[]{:S(2)}, u32[]{:S(2)}) collective-permute-start(bf16[3,512,133]{1,2,0:T(8,128)(2,1)} %copy.89), channel_id=1, source_target_pairs={{0,8},{8,16},{16,24},{1,9},{9,17},{17,25},{2,10},{10,18},{18,26},{... | collective-permute-start | bytes 1225736 | tf_op jit(solution)/shard_map/ppermute | solution.py:13
  17.8 1.0 copy.90
  18.8 3.4 %collective-permute-start.1 = (bf16[3,512,133]{1,2,0:T(8,128)(2,1)}, bf16[3,512,133]{1,2,0:T(8,128)(2,1)S(1)}, u32[]{:S(2)}, u32[]{:S(2)}) collective-permute-start(bf16[3,512,133]{1,2,0:T(8,128)(2,1)} %copy.90), channel_id=1, source_target_pairs={{8,0},{16,8},{24,16},{9,1},{17,9},{25,17},{10,2},{18,10},{26,18},{... | collective-permute-start | bytes 1225736 | tf_op jit(solution)/shard_map/ppermute | solution.py:16
  22.3 1.9 collective-permute-start.3
  24.3 0.3 rev.6
  24.6 0.4 rev.7
  25.0 0.9 copy.68
  25.8 7.5 %collective-permute-done = bf16[3,512,133]{1,2,0:T(8,128)(2,1)S(1)} collective-permute-done((bf16[3,512,133]{1,2,0:T(8,128)(2,1)}, bf16[3,512,133]{1,2,0:T(8,128)(2,1)S(1)}, u32[]{:S(2)}, u32[]{:S(2)}) %collective-permute-start) | collective-permute-done | bytes 408608 | tf_op jit(solution)/shard_map/ppermute | solution.py:13
  33.4 1.2 copy.60
  34.5 0.8 collective-permute-done.1
  35.4 1.2 copy.61
  36.5 0.7 copy-done.12
  37.5 2.6 %pad_maximum_fusion = bf16[3,512,522]{2,1,0:T(8,128)(2,1)S(1)} fusion(bf16[3,512,133]{2,1,0:T(8,128)(2,1)} %copy.61, bf16[3,512,256]{2,1,0:T(8,128)(2,1)} %param.6, bf16[3,512,133]{2,1,0:T(8,128)(2,1)} %copy.60), kind=kLoop, calls=%fused_computation.7 | loop fusion | flops 4810752 | bytes 3207168 | tf_op jit(solution)/shard_map/concatenate | solution.py:17
  40.0 2.2 copy.62
  42.3 2.7 %pad = bf16[1536,1,528]{0,2,1:T(8,128)(2,1)} pad(bf16[1536,1,522]{0,2,1:T(8,128)(2,1)} %copy.62, bf16[]{:T(256)} %constant.12), padding=0_0x0_0x0_6 | pad | bytes 3225602 | tf_op jit(solution)/shard_map/broadcast_in_dim;reshape | solution.py:29
  45.0 1.6 reshape.44
  46.6 0.5 copy.64
  47.3 1.7 convolution_select_fusion
  49.0 1.7 fusion.34
  50.7 0.6 copy.69
  51.4 1.1 reshape.50
  52.5 1.9 copy.70
  54.4 1.1 reshape.52
  55.5 1.9 copy.65
  57.4 1.1 reshape.48
  58.5 0.6 copy.66
  59.2 2.3 reshape.75
  61.5 1.2 copy-done.7
  62.7 1.9 slice_bitcast_fusion
  64.7 21.2 %fusion.36 = f32[1,512,389]{1,0,2:T(1,128)S(1)} fusion(f32[1,528,512]{2,0,1:T(1,128)S(1)} %copy-done.9, f32[512,1,128]{0,1,2:T(1,128)S(1)} %copy-done.13), kind=kOutput, calls=%fused_computation.57 | convolution fusion | flops 305922048 | bytes 2140160 | tf_op jit(solution)/shard_map/conv_general_dilated | solution.py:28
  85.9 0.3 fusion.17
  86.2 0.9 copy-done.4
  87.1 0.8 fusion.26
  88.0 4.2 %fusion.37 = f32[512,1024]{0,1:T(8,128)} fusion(bf16[512,1024]{1,0:T(8,128)(2,1)S(1)} %copy-done, bf16[1024,1024]{0,1:T(8,128)(2,1)} %all-gather.5.cloned.1.call-done), kind=kOutput, calls=%fused_computation.58 | convolution fusion | flops 1073741824 | bytes 5242880 | tf_op jit(solution)/shard_map/dot_general | solution.py:64
  92.3 0.3 reduce-scatter.3.cloned.1.call-start
  92.6 29.9 %all-gather.3.cloned.1.call-done = bf16[512,1024]{0,1:T(8,128)(2,1)} async-done(((bf16[512,256]{0,1:T(8,128)(2,1)}), bf16[512,1024]{0,1:T(8,128)(2,1)}) %all-gather.3.cloned.1.call-update) | async-done | bytes 1048592 | tf_op jit(solution)/shard_map/all_gather | solution.py:77
  122.5 4.4 %convolution_bitcast_fusion = f32[1024,1024]{0,1:T(8,128)} fusion(bf16[512,1024]{0,1:T(8,128)(2,1)} %all-gather.3.cloned.1.call-done, bf16[512,1024]{1,0:T(8,128)(2,1)S(1)} %copy-done), kind=kOutput, calls=%fused_computation.6 | convolution fusion | flops 1073741824 | bytes 6291456 | tf_op jit(solution)/shard_map/dot_general | solution.py:78
  126.9 6.7 %reshape.36 = f32[2,512,4,256]{1,0,3,2:T(2,128)} reshape(f32[1024,1024]{0,1:T(8,128)} %convolution_bitcast_fusion) | data formatting | bytes 8388608 | tf_op jit(solution)/shard_map/reshape | solution.py:84
  133.6 7.3 %copy.71 = f32[2,4,512,256]{3,2,1,0:T(8,128)} copy(f32[2,4,512,256]{2,0,3,1:T(2,128)} %bitcast.71) | data formatting | bytes 8388608 | tf_op jit(solution)/shard_map/transpose | solution.py:85
  140.9 0.9 copy-done.11
  142.0 18.7 %reduce-scatter.5.cloned.1.call-done = f32[512,256]{0,1:T(8,128)} async-done(((f32[512,1024]{0,1:T(8,128)}), f32[512,256]{0,1:T(8,128)}) %reduce-scatter.5.cloned.1.call-update) | async-done | bytes 524304 | tf_op jit(solution)/shard_map/reduce_scatter | solution.py:65
  160.7 1.0 slice.138
  161.6 3.4 %collective-permute-start.4 = (bf16[512,133]{0,1:T(8,128)(2,1)S(1)}, bf16[512,133]{0,1:T(8,128)(2,1)S(1)}, u32[]{:S(2)}, u32[]{:S(2)}) collective-permute-start(bf16[512,133]{0,1:T(8,128)(2,1)S(1)} %slice.138), channel_id=1, source_target_pairs={{8,0},{16,8},{24,16},{9,1},{17,9},{25,17},{10,2},{18,10},{26,18},{... | collective-permute-start | bytes 408584 | tf_op jit(solution)/shard_map/ppermute | solution.py:24
  165.0 4.7 %reduce-precision_reduce_fusion = bf16[512,1024]{1,0:T(8,128)(2,1)} fusion(bf16[512,4,256]{0,2,1:T(8,128)(2,1)} %bitcast.83, bf16[1024,4,256]{0,2,1:T(8,128)(2,1)} %bitcast.82), kind=kOutput, calls=%fused_computation | convolution fusion | flops 1079508992 | bytes 4194304 | tf_op jit(solution)/shard_map/dot_general | solution.py:95
  169.9 1.1 copy-done.3
  171.1 5.4 %fusion.18 = f32[1,512,262]{1,0,2:T(1,128)S(1)} fusion(f32[512,1,128]{0,1,2:T(1,128)S(1)} %copy.75, f32[1,512,389]{1,2,0:T(8,128)S(1)} %bitcast.73), kind=kOutput, calls=%fused_computation.32 | convolution fusion | flops 206045184 | bytes 1595392 | tf_op jit(solution)/shard_map/conv_general_dilated | solution.py:28
  176.6 0.3 fusion.24
  177.0 1.1 copy.76
  178.1 2.4 reshape.69
  180.4 2.7 %pad.2 = f32[1536,1,264]{0,2,1:T(8,128)} pad(f32[1536,1,262]{0,2,1:T(8,128)} %reshape.69, f32[]{:T(128)} %constant.11.clone.1), padding=0_0x0_0x0_2 | pad | bytes 3231748 | tf_op jit(solution)/shard_map/broadcast_in_dim;reshape | solution.py:29
  183.2 3.2 %reshape.55 = f32[1536,1,8,33]{0,1,3,2:T(1,128)S(1)} reshape(f32[1536,1,264]{0,2,1:T(8,128)} %pad.2) | data formatting | bytes 3244032 | tf_op jit(solution)/shard_map/conv_general_dilated | solution.py:28
  186.6 0.5 copy-done.17
  187.1 1.5 fusion.1
  188.6 0.3 copy.80
  188.9 0.3 reshape.59
  189.2 23.6 %reduce-scatter.3.cloned.1.call-done = f32[512,256]{1,0:T(8,128)} async-done(((f32[4096,256]{1,0:T(8,128)}), f32[512,256]{1,0:T(8,128)}) %reduce-scatter.3.cloned.1.call-update) | async-done | bytes 524304 | tf_op jit(solution)/shard_map/reduce_scatter | solution.py:88
  212.8 1.2 convert_element_type.21
  213.9 1.9 collective-permute-start.2
  215.9 1.2 copy.81
  217.1 17.6 %collective-permute-done.2 = bf16[512,256]{1,0:T(8,128)(2,1)S(1)} collective-permute-done((bf16[512,256]{1,0:T(8,128)(2,1)S(1)}, bf16[512,256]{1,0:T(8,128)(2,1)S(1)}, u32[]{:S(2)}, u32[]{:S(2)}) %collective-permute-start.2) | collective-permute-done | bytes 262176 | tf_op jit(solution)/shard_map/ppermute | solution.py:93
  234.7 0.7 copy.102
  (53 shorter events, 1.8 us)
Async XLA Ops:
  7.2 80.8 %copy-start = (bf16[512,1024]{1,0:T(8,128)(2,1)S(1)}, bf16[512,1024]{1,0:T(8,128)(2,1)}, u32[]{:S(2)}) copy-start(bf16[512,1024]{1,0:T(8,128)(2,1)} %param.10) | copy-start | bytes 3145732
  7.2 15.0 %all-to-all-start = ((bf16[4,128,256]{2,1,0:T(8,128)(2,1)}), bf16[4,128,256]{2,1,0:T(8,128)(2,1)S(1)}, u32[]{:S(2)}, u32[]{:S(2)}) async-start(bf16[4,128,256]{2,1,0:T(8,128)(2,1)} %bitcast.78), calls=%async_computation.1 | async-start | bytes 524288 | tf_op jit(solution)/shard_map/all_to_all | solution.py:43
  11.5 76.5 %all-gather.5.cloned.1.call-start = ((), (), s32[]{:S(2)}) async-start(), calls=%async_computation.5 | async-start | bytes 2359296 | tf_op jit(solution)/shard_map/all_gather | solution.py:51
  13.4 10.9 %copy-start.14 = (f32[3,512,7]{1,2,0:T(8,128)S(1)}, f32[3,512,7]{1,2,0:T(8,128)}, u32[]{:S(2)}) copy-start(f32[3,512,7]{1,2,0:T(8,128)} %param.7) | copy-start | bytes 129028
  13.4 11.2 %copy-start.10 = (f32[512,128]{1,0:T(8,128)S(1)}, f32[512,128]{1,0:T(8,128)}, u32[]{:S(2)}) copy-start(f32[512,128]{1,0:T(8,128)} %param.8) | copy-start | bytes 786436
  14.4 19.0 %collective-permute-start = (bf16[3,512,133]{1,2,0:T(8,128)(2,1)}, bf16[3,512,133]{1,2,0:T(8,128)(2,1)S(1)}, u32[]{:S(2)}, u32[]{:S(2)}) collective-permute-start(bf16[3,512,133]{1,2,0:T(8,128)(2,1)} %copy.89), channel_id=1, source_target_pairs={{0,8},{8,16},{16,24},{1,9},{9,17},{17,25},{2,10},{10,18},{18,26},{... | collective-permute-start | bytes 1225736 | tf_op jit(solution)/shard_map/ppermute | solution.py:13
  18.8 16.6 %collective-permute-start.1 = (bf16[3,512,133]{1,2,0:T(8,128)(2,1)}, bf16[3,512,133]{1,2,0:T(8,128)(2,1)S(1)}, u32[]{:S(2)}, u32[]{:S(2)}) collective-permute-start(bf16[3,512,133]{1,2,0:T(8,128)(2,1)} %copy.90), channel_id=1, source_target_pairs={{8,0},{16,8},{24,16},{9,1},{17,9},{25,17},{10,2},{18,10},{26,18},{... | collective-permute-start | bytes 1225736 | tf_op jit(solution)/shard_map/ppermute | solution.py:16
  22.3 14.2 %collective-permute-start.3 = (bf16[128,1024]{0,1:T(8,128)(2,1)S(1)}, bf16[128,1024]{0,1:T(8,128)(2,1)S(1)}, u32[]{:S(2)}, u32[]{:S(2)}) collective-permute-start(bf16[128,1024]{0,1:T(8,128)(2,1)S(1)} %bitcast.79), channel_id=1, source_target_pairs={{0,0},{1,4},{2,8},{3,12},{4,16},{5,20},{6,24},{7,28},{8,1},{9,5},{... | collective-permute-start | bytes 786440 | tf_op jit(solution)/shard_map/ppermute | solution.py:50
  36.5 0.7 copy-start.12
  37.3 85.2 %all-gather.3.cloned.1.call-start = ((), (), s32[]{:S(2)}) async-start(), calls=%async_computation.3 | async-start | bytes 1310720 | tf_op jit(solution)/shard_map/all_gather | solution.py:77
  46.6 0.7 copy-start.16
  59.2 2.3 copy-start.6
  61.5 1.2 copy-start.7
  62.7 23.5 %copy-start.2 = (f32[512,516]{0,1:T(8,128)}, f32[512,516]{0,1:T(8,128)S(1)}, u32[]{:S(2)}) copy-start(f32[512,516]{0,1:T(8,128)S(1)} %slice_bitcast_fusion.2) | copy-start | bytes 3170308
  62.7 2.0 copy-start.9
  62.7 2.0 copy-start.13
  64.7 21.2 %copy-start.15 = (f32[512]{0:T(512)S(1)}, f32[512]{0:T(512)}, u32[]{:S(2)}) copy-start(f32[512]{0:T(512)} %param.9) | copy-start | bytes 6148
  86.2 0.9 copy-start.4
  87.9 72.7 %reduce-scatter.5.cloned.1.call-start = ((), (), s32[]{:S(2)}) async-start(), calls=%async_computation.6 | async-start | bytes 2621440 | tf_op jit(solution)/shard_map/reduce_scatter | solution.py:65
  92.3 120.5 %reduce-scatter.3.cloned.1.call-start = ((), (), s32[]{:S(2)}) async-start(), calls=%async_computation.4 | async-start | bytes 4718592 | tf_op jit(solution)/shard_map/reduce_scatter | solution.py:88
  140.8 1.0 copy-start.11
  161.6 8.1 %collective-permute-start.4 = (bf16[512,133]{0,1:T(8,128)(2,1)S(1)}, bf16[512,133]{0,1:T(8,128)(2,1)S(1)}, u32[]{:S(2)}, u32[]{:S(2)}) collective-permute-start(bf16[512,133]{0,1:T(8,128)(2,1)S(1)} %slice.138), channel_id=1, source_target_pairs={{8,0},{16,8},{24,16},{9,1},{17,9},{25,17},{10,2},{18,10},{26,18},{... | collective-permute-start | bytes 408584 | tf_op jit(solution)/shard_map/ppermute | solution.py:24
  165.0 4.7 %copy-start.5 = (f32[512,389]{0,1:T(8,128)S(1)}, f32[512,389]{0,1:T(8,128)}, u32[]{:S(2)}) copy-start(f32[512,389]{0,1:T(8,128)} %copy-done.4) | copy-start | bytes 2390020
  165.0 4.7 %copy-start.8 = (f32[512,256]{0,1:T(8,128)S(1)}, f32[512,256]{0,1:T(8,128)}, u32[]{:S(2)}) copy-start(f32[512,256]{0,1:T(8,128)} %reduce-scatter.5.cloned.1.call-done) | copy-start | bytes 1572868
  169.7 1.2 copy-start.3
  186.4 0.7 copy-start.17
  212.8 22.6 %copy-start.1 = (bf16[512,1024]{1,0:T(8,128)(2,1)S(1)}, bf16[512,1024]{1,0:T(8,128)(2,1)}, u32[]{:S(2)}) copy-start(bf16[512,1024]{1,0:T(8,128)(2,1)} %param.10) | copy-start | bytes 3145732
  213.9 20.7 %collective-permute-start.2 = (bf16[512,256]{1,0:T(8,128)(2,1)S(1)}, bf16[512,256]{1,0:T(8,128)(2,1)S(1)}, u32[]{:S(2)}, u32[]{:S(2)}) collective-permute-start(bf16[512,256]{1,0:T(8,128)(2,1)S(1)} %convert_element_type.21), channel_id=1, source_target_pairs={{0,0},{1,8},{2,16},{3,24},{4,1},{5,9},{6,17},{7,25},{8,2},{9,10},{... | collective-permute-start | bytes 786440 | tf_op jit(solution)/shard_map/ppermute | solution.py:93
Sparse Core Ops, SparseCore 0:
  37.4 38.2 all-gather.4
  88.1 34.3 all-gather.2
  125.4 35.1 reduce-scatter.4
  162.8 49.9 reduce-scatter.2
where the time goes:
time: 243 us; the launch traced here: 242 us
  waiting for transfers between devices  98.2 us (40%)
  local copies, waits for them, and re-layouts  60.3 us (25%)
  matrix products  43.1 us (18%)
  starting transfers between devices  18.8 us (8%)
  between operations  14.2 us (6%)
  other arithmetic  7.25 us (3%)
    all_gather x1, waiting for transfers between devices, shards(): gated_all = lax.all_gather(gated, 'seq', axis=1, tiled=True)  29.9 us
    conv_general_dilated x4, matrix products, correlate(): lax.conv_general_dilated(signal[None], taps[:, None, :], (1,), 'VALID', d...  29.8 us
    reduce_scatter x1, waiting for transfers between devices, shards(): lax.psum_scatter(partial_out, 'tp', scatter_dimension=0, tiled=True)  23.6 us
    reduce_scatter x1, waiting for transfers between devices, shards(): lax.psum_scatter(partial_grad, 'seq', scatter_dimension=1, tiled=True)  18.7 us
    ppermute x1, waiting for transfers between devices, shards(): mixed = lax.ppermute(output_sum.astype(jnp.bfloat16), ('seq', 'tp'), route)  17.6 us
    conv_general_dilated x12, local copies, waits for them, and re-layouts, correlate(): lax.conv_general_dilated(signal[None], taps[:, None, :], (1,), 'VALID', d...  13.3 us
    another operation x4, local copies, waits for them, and re-layouts, correlate(): signal[None]  9.99 us
    unnamed x39, local copies, waits for them, and re-layouts  8.37 us
  transfers between devices with their start and end apart: 10, of which 6 were waited for; matrix products, arithmetic and copies ran while one was open for 43% of the time, Pallas kernels for 0%

commit v1 on v0

--- a/solution.py
+++ b/solution.py
@@ -3,6 +3,17 @@
 import jax.numpy as jnp
 from jax import lax
 from jax.sharding import PartitionSpec as P
+
+
+def collect(x, axis, dim):
+    ways = lax.axis_size(axis)
+    pieces = [x]
+    for far in range(1, ways):
+        pieces.append(
+            lax.ppermute(pieces[far - 1], axis, [(d, (d - 1) % ways) for d in range(ways)])
+        )
+    line = jnp.concatenate(pieces, axis=dim)
+    return jnp.roll(line, lax.axis_index(axis) * x.shape[dim], axis=dim)
 
 
 def extended(block, sides, width):
@@ -74,7 +85,7 @@
     summed = convolved + skip_gain[:, None] * product[:, taps_long - 1 :]
     query_tail = query_feat[:, taps_long - 1 :]
     gated = (query_tail[:, :length] * summed[:, :length]).astype(jnp.bfloat16)
-    gated_all = lax.all_gather(gated, "seq", axis=1, tiled=True)
+    gated_all = collect(gated, "seq", 1)
     partial_out = lax.dot_general(
         out_weight, gated_all, (((0,), (0,)), ((), ())), preferred_element_type=jnp.float32
     )

time: 243 us -> 249 us (1.025)
  waiting for transfers between devices: 98.2 us -> 81.3 us
  local copies, waits for them, and re-layouts: 60.3 us -> 69.4 us
  blocking collectives: 0 us -> 8.98 us
  starting transfers between devices: 18.8 us -> 24.4 us
    all_gather x1 -> x0, waiting for transfers between devices: 29.9 us -> none  [shards(): gated_all = lax.all_gather(gated, 'seq', axis=1, tiled=True)]
    ppermute x0 -> x3, waiting for transfers between devices: none -> 19.2 us  [collect(): lax.ppermute(pieces[far - 1], axis, [(d, (d - 1) % ways) for d in range(w...]
    reduce_scatter x1, waiting for transfers between devices: 18.7 us -> 0.02 us  [shards(): lax.psum_scatter(partial_grad, 'seq', scatter_dimension=1, tiled=True)]
    all_to_all x0 -> x1, blocking collectives: none -> 8.98 us  [rows_of_slab(): mine = lax.all_to_all(split, 'seq', 0, 0)]
    ppermute x1, waiting for transfers between devices: 0.01 us -> 8.07 us  [rows_of_slab(): moved = lax.ppermute(mine, ('seq', 'tp'), route)]
    unnamed x39 -> x47, local copies, waits for them, and re-layouts: 8.37 us -> 14.8 us
    ppermute x1, waiting for transfers between devices: 0.83 us -> 6.56 us  [extended(): lax.ppermute(lax.slice_in_dim(block, 0, width, axis=dim), axis, backward)]
    ppermute x0 -> x3, starting transfers between devices: none -> 5.34 us  [collect(): lax.ppermute(pieces[far - 1], axis, [(d, (d - 1) % ways) for d in range(w...]
  transfers between devices with their start and end apart: 10 -> 11, of which waited for: 6 -> 8; matrix products, arithmetic and copies ran while one was open for 43% -> 44% of each run, Pallas kernels for 0% -> 0%
where the time goes in v1:
time: 249 us; the launch traced here: 248 us
  waiting for transfers between devices  81.3 us (33%)
  local copies, waits for them, and re-layouts  69.4 us (28%)
  matrix products  41.9 us (17%)
  starting transfers between devices  24.4 us (10%)
  between operations  14.2 us (6%)
  blocking collectives  8.98 us (4%)
  other arithmetic  7.46 us (3%)
    conv_general_dilated x4, matrix products, correlate(): lax.conv_general_dilated(signal[None], taps[:, None, :], (1,), 'VALID', d...  29.7 us
    reduce_scatter x1, waiting for transfers between devices, shards(): lax.psum_scatter(partial_out, 'tp', scatter_dimension=0, tiled=True)  23.5 us
    ppermute x3, waiting for transfers between devices, collect(): lax.ppermute(pieces[far - 1], axis, [(d, (d - 1) % ways) for d in range(w...  19.2 us
    ppermute x1, waiting for transfers between devices, shards(): mixed = lax.ppermute(output_sum.astype(jnp.bfloat16), ('seq', 'tp'), route)  17.6 us
    unnamed x47, local copies, waits for them, and re-layouts  14.8 us
    conv_general_dilated x12, local copies, waits for them, and re-layouts, correlate(): lax.conv_general_dilated(signal[None], taps[:, None, :], (1,), 'VALID', d...  12.1 us
    another operation x4, local copies, waits for them, and re-layouts, correlate(): signal[None]  10 us
    all_to_all x1, blocking collectives, rows_of_slab(): mine = lax.all_to_all(split, 'seq', 0, 0)  8.98 us
  transfers between devices with their start and end apart: 11, of which 8 were waited for; matrix products, arithmetic and copies ran while one was open for 44% of the time, Pallas kernels for 0%

profile of v1, /device:TPU:4, one launch (start us, length us, event | category | flops | bytes accessed | tf_op | source)
XLA Modules:
  0.0 247.7 jit_solution(3066382628281024608)
XLA Ops:
  7.2 9.0 %all_to_all.5 = bf16[4,128,256]{2,1,0:T(8,128)(2,1)S(1)} all-to-all(bf16[4,128,256]{2,1,0:T(8,128)(2,1)} %bitcast.79), channel_id=1, replica_groups=mesh['seq'=4,'tp'=8] {'seq'}, dimensions={0} | all-to-all | bytes 524288 | tf_op jit(solution)/shard_map/all_to_all | solution.py:54
  16.4 4.0 %collective-permute-start.6 = (bf16[128,1024]{0,1:T(8,128)(2,1)S(1)}, bf16[128,1024]{0,1:T(8,128)(2,1)S(1)}, u32[]{:S(2)}, u32[]{:S(2)}) collective-permute-start(bf16[128,1024]{0,1:T(8,128)(2,1)S(1)} %bitcast.80), channel_id=1, source_target_pairs={{0,0},{1,4},{2,8},{3,12},{4,16},{5,20},{6,24},{7,28},{8,1},{9,5},{... | collective-permute-start | bytes 786440 | tf_op jit(solution)/shard_map/ppermute | solution.py:61
  20.4 8.1 %collective-permute-done.6 = bf16[128,1024]{0,1:T(8,128)(2,1)S(1)} collective-permute-done((bf16[128,1024]{0,1:T(8,128)(2,1)S(1)}, bf16[128,1024]{0,1:T(8,128)(2,1)S(1)}, u32[]{:S(2)}, u32[]{:S(2)}) %collective-permute-start.6) | collective-permute-done | bytes 262176 | tf_op jit(solution)/shard_map/ppermute | solution.py:61
  28.5 0.7 copy-done.13
  29.7 1.0 copy.89
  30.7 6.0 %collective-permute-start.1 = (bf16[3,512,133]{1,2,0:T(8,128)(2,1)}, bf16[3,512,133]{1,2,0:T(8,128)(2,1)S(1)}, u32[]{:S(2)}, u32[]{:S(2)}) collective-permute-start(bf16[3,512,133]{1,2,0:T(8,128)(2,1)} %copy.89), channel_id=1, source_target_pairs={{8,0},{16,8},{24,16},{9,1},{17,9},{25,17},{10,2},{18,10},{26,18},{... | collective-permute-start | bytes 1225736 | tf_op jit(solution)/shard_map/ppermute | solution.py:27
  37.0 1.9 collective-permute-start
  39.6 0.9 copy.67
  40.5 6.6 %collective-permute-done.1 = bf16[3,512,133]{1,2,0:T(8,128)(2,1)S(1)} collective-permute-done((bf16[3,512,133]{1,2,0:T(8,128)(2,1)}, bf16[3,512,133]{1,2,0:T(8,128)(2,1)S(1)}, u32[]{:S(2)}, u32[]{:S(2)}) %collective-permute-start.1) | collective-permute-done | bytes 408608 | tf_op jit(solution)/shard_map/ppermute | solution.py:27
  47.1 1.2 copy.60
  48.2 6.3 %collective-permute-done = bf16[3,512,133]{1,2,0:T(8,128)(2,1)S(1)} collective-permute-done((bf16[3,512,133]{1,2,0:T(8,128)(2,1)S(1)}, bf16[3,512,133]{1,2,0:T(8,128)(2,1)S(1)}, u32[]{:S(2)}, u32[]{:S(2)}) %collective-permute-start) | collective-permute-done | bytes 408608 | tf_op jit(solution)/shard_map/ppermute | solution.py:24
  54.5 1.2 copy.59
  55.6 2.6 %pad_maximum_fusion = bf16[3,512,522]{2,1,0:T(8,128)(2,1)S(1)} fusion(bf16[3,512,133]{2,1,0:T(8,128)(2,1)} %copy.60, bf16[3,512,256]{2,1,0:T(8,128)(2,1)} %param.6, bf16[3,512,133]{2,1,0:T(8,128)(2,1)} %copy.59), kind=kLoop, calls=%fused_computation.7 | loop fusion | flops 4810752 | bytes 3207168 | tf_op jit(solution)/shard_map/concatenate | solution.py:28
  58.2 2.2 copy.61
  60.5 2.7 %pad = bf16[1536,1,528]{0,2,1:T(8,128)(2,1)} pad(bf16[1536,1,522]{0,2,1:T(8,128)(2,1)} %copy.61, bf16[]{:T(256)} %constant.41), padding=0_0x0_0x0_6 | pad | bytes 3225602 | tf_op jit(solution)/shard_map/broadcast_in_dim;reshape | solution.py:40
  63.2 1.6 reshape.44
  65.5 1.7 convolution_select_fusion
  67.2 1.8 fusion.35
  69.0 0.6 copy.64
  69.6 1.1 reshape.48
  70.7 1.9 copy.65
  72.6 2.3 reshape.75
  74.9 1.9 copy.69
  76.7 1.1 reshape.52
  78.5 1.1 reshape.50
  79.7 1.7 slice_bitcast_fusion
  81.4 4.2 %fusion.38 = f32[512,1024]{0,1:T(8,128)} fusion(bf16[512,1024]{1,0:T(8,128)(2,1)S(1)} %copy-done, bf16[1024,1024]{0,1:T(8,128)(2,1)} %all-gather.2.cloned.1.call-done), kind=kOutput, calls=%fused_computation.67 | convolution fusion | flops 1073741824 | bytes 5242880 | tf_op jit(solution)/shard_map/dot_general | solution.py:75
  85.7 1.4 slice_bitcast_fusion.2
  87.3 21.1 %fusion.37 = f32[1,512,389]{1,0,2:T(1,128)S(1)} fusion(f32[1,528,512]{2,0,1:T(1,128)S(1)} %copy-done.8, f32[512,1,128]{0,1,2:T(1,128)S(1)} %copy-done.14), kind=kOutput, calls=%fused_computation.66 | convolution fusion | flops 305922048 | bytes 2140160 | tf_op jit(solution)/shard_map/conv_general_dilated | solution.py:39
  108.7 1.0 constant_dynamic-update-slice_fusion.7
  109.7 11.9 %collective-permute-done.2 = bf16[512,256]{0,1:T(8,128)(2,1)S(1)} collective-permute-done((bf16[512,256]{0,1:T(8,128)(2,1)S(1)}, bf16[512,256]{0,1:T(8,128)(2,1)S(1)}, u32[]{:S(2)}, u32[]{:S(2)}) %collective-permute-start.2) | collective-permute-done | bytes 262176 | tf_op jit(solution)/shard_map/ppermute | solution.py:13
  121.6 1.9 collective-permute-start.3
  123.5 5.3 %collective-permute-done.3 = bf16[512,256]{0,1:T(8,128)(2,1)} collective-permute-done((bf16[512,256]{0,1:T(8,128)(2,1)S(1)}, bf16[512,256]{0,1:T(8,128)(2,1)}, u32[]{:S(2)}, u32[]{:S(2)}) %collective-permute-start.3) | collective-permute-done | bytes 262176 | tf_op jit(solution)/shard_map/ppermute | solution.py:13
  128.8 3.5 %collective-permute-start.4 = (bf16[512,256]{0,1:T(8,128)(2,1)}, bf16[512,256]{0,1:T(8,128)(2,1)}, u32[]{:S(2)}, u32[]{:S(2)}) collective-permute-start(bf16[512,256]{0,1:T(8,128)(2,1)} %collective-permute-done.3), channel_id=1, source_target_pairs={{0,24},{8,0},{16,8},{24,16},{1,25},{9,1},{17,9},{25,17},{2,26},{10... | collective-permute-start | bytes 786440 | tf_op jit(solution)/shard_map/ppermute | solution.py:13
  132.3 0.7 constant_dynamic-update-slice_fusion.6
  133.0 1.7 constant_dynamic-update-slice_fusion.5
  134.7 2.0 collective-permute-done.4
  136.7 1.7 constant_dynamic-update-slice_fusion.4
  138.4 1.7 constant_dynamic-update-slice_fusion.3
  140.1 0.7 constant_dynamic-update-slice_fusion.2
  140.8 1.7 constant_dynamic-update-slice_fusion.1
  142.5 1.7 constant_dynamic-update-slice_fusion
  144.2 1.3 constant_dynamic-slice_fusion
  145.5 1.0 copy-done.9
  146.5 3.2 %convolution_bitcast_fusion = f32[1024,1024]{0,1:T(8,128)} fusion(bf16[512,1024]{0,1:T(8,128)(2,1)S(1)} %constant_dynamic-slice_fusion, bf16[512,1024]{1,0:T(8,128)(2,1)S(1)} %copy-done), kind=kOutput, calls=%fused_computation.6 | convolution fusion | flops 1073741824 | bytes 6291456 | tf_op jit(solution)/shard_map/dot_general | solution.py:89
  149.7 6.7 %reshape.36 = f32[2,512,4,256]{1,0,3,2:T(2,128)} reshape(f32[1024,1024]{0,1:T(8,128)} %convolution_bitcast_fusion) | data formatting | bytes 8388608 | tf_op jit(solution)/shard_map/reshape | solution.py:95
  156.4 7.2 %copy.70 = f32[2,4,512,256]{3,2,1,0:T(8,128)} copy(f32[2,4,512,256]{2,0,3,1:T(2,128)} %bitcast.71) | data formatting | bytes 8388608 | tf_op jit(solution)/shard_map/transpose | solution.py:96
  163.6 0.9 copy-done.11
  164.7 1.0 slice.138
  165.7 5.1 %collective-permute-start.7 = (bf16[512,133]{0,1:T(8,128)(2,1)S(1)}, bf16[512,133]{0,1:T(8,128)(2,1)S(1)}, u32[]{:S(2)}, u32[]{:S(2)}) collective-permute-start(bf16[512,133]{0,1:T(8,128)(2,1)S(1)} %slice.138), channel_id=1, source_target_pairs={{8,0},{16,8},{24,16},{9,1},{17,9},{25,17},{10,2},{18,10},{26,18},{... | collective-permute-start | bytes 408584 | tf_op jit(solution)/shard_map/ppermute | solution.py:35
  170.8 4.7 %reduce-precision_reduce_fusion = bf16[512,1024]{1,0:T(8,128)(2,1)} fusion(bf16[512,4,256]{0,2,1:T(8,128)(2,1)} %bitcast.74, bf16[1024,4,256]{0,2,1:T(8,128)(2,1)} %bitcast.83), kind=kOutput, calls=%fused_computation | convolution fusion | flops 1079508992 | bytes 4194304 | tf_op jit(solution)/shard_map/dot_general | solution.py:106
  175.6 1.1 copy-done.4
  176.9 5.4 %fusion.18 = f32[1,512,262]{1,0,2:T(1,128)S(1)} fusion(f32[512,1,128]{0,1,2:T(1,128)S(1)} %copy.74, f32[1,512,389]{1,2,0:T(8,128)S(1)} %bitcast.73), kind=kOutput, calls=%fused_computation.32 | convolution fusion | flops 206045184 | bytes 1595392 | tf_op jit(solution)/shard_map/conv_general_dilated | solution.py:39
  182.8 1.1 copy.75
  183.9 2.4 reshape.69
  186.2 2.7 %pad.2 = f32[1536,1,264]{0,2,1:T(8,128)} pad(f32[1536,1,262]{0,2,1:T(8,128)} %reshape.69, f32[]{:T(128)} %constant.40.clone.1), padding=0_0x0_0x0_2 | pad | bytes 3231748 | tf_op jit(solution)/shard_map/broadcast_in_dim;reshape | solution.py:40
  188.9 3.2 %reshape.55 = f32[1536,1,8,33]{0,1,3,2:T(1,128)S(1)} reshape(f32[1536,1,264]{0,2,1:T(8,128)} %pad.2) | data formatting | bytes 3244032 | tf_op jit(solution)/shard_map/conv_general_dilated | solution.py:39
  192.9 1.5 fusion.1
  195.0 23.5 %reduce-scatter.3.cloned.1.call-done = f32[512,256]{1,0:T(8,128)} async-done(((f32[4096,256]{1,0:T(8,128)}), f32[512,256]{1,0:T(8,128)}) %reduce-scatter.3.cloned.1.call-update) | async-done | bytes 524304 | tf_op jit(solution)/shard_map/reduce_scatter | solution.py:99
  218.5 1.2 convert_element_type.21
  219.7 1.9 collective-permute-start.5
  221.7 1.2 copy.80
  222.8 17.6 %collective-permute-done.5 = bf16[512,256]{1,0:T(8,128)(2,1)S(1)} collective-permute-done((bf16[512,256]{1,0:T(8,128)(2,1)S(1)}, bf16[512,256]{1,0:T(8,128)(2,1)S(1)}, u32[]{:S(2)}, u32[]{:S(2)}) %collective-permute-start.5) | collective-permute-done | bytes 262176 | tf_op jit(solution)/shard_map/ppermute | solution.py:104
  240.4 0.7 copy.108
  (65 shorter events, 5.7 us)
Async XLA Ops:
  7.2 74.3 %copy-start = (bf16[512,1024]{1,0:T(8,128)(2,1)S(1)}, bf16[512,1024]{1,0:T(8,128)(2,1)}, u32[]{:S(2)}) copy-start(bf16[512,1024]{1,0:T(8,128)(2,1)} %param.10) | copy-start | bytes 3145732
  7.2 22.1 %copy-start.2 = (bf16[3,512,256]{2,1,0:T(8,128)(2,1)S(1)}, bf16[3,512,256]{2,1,0:T(8,128)(2,1)}, u32[]{:S(2)}) copy-start(bf16[3,512,256]{2,1,0:T(8,128)(2,1)} %param.6) | copy-start | bytes 2359300
  7.2 74.2 %all-gather.2.cloned.1.call-start = ((), (), s32[]{:S(2)}) async-start(), calls=%async_computation.4 | async-start | bytes 2359296 | tf_op jit(solution)/shard_map/all_gather | solution.py:62
  16.4 12.1 %collective-permute-start.6 = (bf16[128,1024]{0,1:T(8,128)(2,1)S(1)}, bf16[128,1024]{0,1:T(8,128)(2,1)S(1)}, u32[]{:S(2)}, u32[]{:S(2)}) collective-permute-start(bf16[128,1024]{0,1:T(8,128)(2,1)S(1)} %bitcast.80), channel_id=1, source_target_pairs={{0,0},{1,4},{2,8},{3,12},{4,16},{5,20},{6,24},{7,28},{8,1},{9,5},{... | collective-permute-start | bytes 786440 | tf_op jit(solution)/shard_map/ppermute | solution.py:61
  28.5 0.7 copy-start.13
  29.2 135.5 %reduce-scatter.5.cloned.1.call-start = ((), (), s32[]{:S(2)}) async-start(), calls=%async_computation.5 | async-start | bytes 2621440 | tf_op jit(solution)/shard_map/reduce_scatter | solution.py:76
  29.7 9.2 %copy-start.15 = (f32[3,512,7]{1,2,0:T(8,128)S(1)}, f32[3,512,7]{1,2,0:T(8,128)}, u32[]{:S(2)}) copy-start(f32[3,512,7]{1,2,0:T(8,128)} %param.7) | copy-start | bytes 129028
  29.7 9.6 %copy-start.10 = (f32[512,128]{1,0:T(8,128)S(1)}, f32[512,128]{1,0:T(8,128)}, u32[]{:S(2)}) copy-start(f32[512,128]{1,0:T(8,128)} %param.8) | copy-start | bytes 786436
  30.7 16.4 %collective-permute-start.1 = (bf16[3,512,133]{1,2,0:T(8,128)(2,1)}, bf16[3,512,133]{1,2,0:T(8,128)(2,1)S(1)}, u32[]{:S(2)}, u32[]{:S(2)}) collective-permute-start(bf16[3,512,133]{1,2,0:T(8,128)(2,1)} %copy.89), channel_id=1, source_target_pairs={{8,0},{16,8},{24,16},{9,1},{17,9},{25,17},{10,2},{18,10},{26,18},{... | collective-permute-start | bytes 1225736 | tf_op jit(solution)/shard_map/ppermute | solution.py:27
  37.0 17.5 %collective-permute-start = (bf16[3,512,133]{1,2,0:T(8,128)(2,1)S(1)}, bf16[3,512,133]{1,2,0:T(8,128)(2,1)S(1)}, u32[]{:S(2)}, u32[]{:S(2)}) collective-permute-start(bf16[3,512,133]{1,2,0:T(8,128)(2,1)S(1)} %copy.88), channel_id=1, source_target_pairs={{0,8},{8,16},{16,24},{1,9},{9,17},{17,25},{2,10},{10,18},{18,26},{... | collective-permute-start | bytes 1225736 | tf_op jit(solution)/shard_map/ppermute | solution.py:24
  64.8 0.7 copy-start.17
  85.7 1.5 copy-start.14
  85.7 132.8 %reduce-scatter.3.cloned.1.call-start = ((), (), s32[]{:S(2)}) async-start(), calls=%async_computation.3 | async-start | bytes 4718592 | tf_op jit(solution)/shard_map/reduce_scatter | solution.py:99
  85.7 1.6 copy-start.8
  87.3 21.4 %copy-start.3 = (f32[512,516]{0,1:T(8,128)}, f32[512,516]{0,1:T(8,128)S(1)}, u32[]{:S(2)}) copy-start(f32[512,516]{0,1:T(8,128)S(1)} %slice_bitcast_fusion.2) | copy-start | bytes 3170308
  87.3 21.1 %copy-start.16 = (f32[512]{0:T(512)S(1)}, f32[512]{0:T(512)}, u32[]{:S(2)}) copy-start(f32[512]{0:T(512)} %param.9) | copy-start | bytes 6148
  108.7 1.0 copy-start.5
  109.7 19.1 %copy-start.12 = (bf16[512,256]{0,1:T(8,128)(2,1)}, bf16[512,256]{0,1:T(8,128)(2,1)S(1)}, u32[]{:S(2)}) copy-start(bf16[512,256]{0,1:T(8,128)(2,1)S(1)} %get-tuple-element.7) | copy-start | bytes 786436
  109.7 11.9 %collective-permute-start.2 = (bf16[512,256]{0,1:T(8,128)(2,1)S(1)}, bf16[512,256]{0,1:T(8,128)(2,1)S(1)}, u32[]{:S(2)}, u32[]{:S(2)}) collective-permute-start(bf16[512,256]{0,1:T(8,128)(2,1)S(1)} %get-tuple-element.7), channel_id=1, source_target_pairs={{0,24},{8,0},{16,8},{24,16},{1,25},{9,1},{17,9},{25,17},{2,26},{10... | collective-permute-start | bytes 786440 | tf_op jit(solution)/shard_map/ppermute | solution.py:13
  121.6 7.2 %collective-permute-start.3 = (bf16[512,256]{0,1:T(8,128)(2,1)S(1)}, bf16[512,256]{0,1:T(8,128)(2,1)}, u32[]{:S(2)}, u32[]{:S(2)}) collective-permute-start(bf16[512,256]{0,1:T(8,128)(2,1)S(1)} %collective-permute-done.2), channel_id=1, source_target_pairs={{0,24},{8,0},{16,8},{24,16},{1,25},{9,1},{17,9},{25,17},{2,26},{10... | collective-permute-start | bytes 786440 | tf_op jit(solution)/shard_map/ppermute | solution.py:13
  128.8 7.9 %collective-permute-start.4 = (bf16[512,256]{0,1:T(8,128)(2,1)}, bf16[512,256]{0,1:T(8,128)(2,1)}, u32[]{:S(2)}, u32[]{:S(2)}) collective-permute-start(bf16[512,256]{0,1:T(8,128)(2,1)} %collective-permute-done.3), channel_id=1, source_target_pairs={{0,24},{8,0},{16,8},{24,16},{1,25},{9,1},{17,9},{25,17},{2,26},{10... | collective-permute-start | bytes 786440 | tf_op jit(solution)/shard_map/ppermute | solution.py:13
  145.5 1.0 copy-start.9
  163.6 0.9 copy-start.11
  165.7 9.8 %collective-permute-start.7 = (bf16[512,133]{0,1:T(8,128)(2,1)S(1)}, bf16[512,133]{0,1:T(8,128)(2,1)S(1)}, u32[]{:S(2)}, u32[]{:S(2)}) collective-permute-start(bf16[512,133]{0,1:T(8,128)(2,1)S(1)} %slice.138), channel_id=1, source_target_pairs={{8,0},{16,8},{24,16},{9,1},{17,9},{25,17},{10,2},{18,10},{26,18},{... | collective-permute-start | bytes 408584 | tf_op jit(solution)/shard_map/ppermute | solution.py:35
  170.8 4.7 %copy-start.6 = (f32[512,389]{0,1:T(8,128)S(1)}, f32[512,389]{0,1:T(8,128)}, u32[]{:S(2)}) copy-start(f32[512,389]{0,1:T(8,128)} %copy-done.5) | copy-start | bytes 2390020
  170.8 4.7 %copy-start.7 = (f32[512,256]{0,1:T(8,128)S(1)}, f32[512,256]{0,1:T(8,128)}, u32[]{:S(2)}) copy-start(f32[512,256]{0,1:T(8,128)} %reduce-scatter.5.cloned.1.call-done) | copy-start | bytes 1572868
  175.5 1.2 copy-start.4
  192.2 0.7 copy-start.18
  218.5 22.6 %copy-start.1 = (bf16[512,1024]{1,0:T(8,128)(2,1)S(1)}, bf16[512,1024]{1,0:T(8,128)(2,1)}, u32[]{:S(2)}) copy-start(bf16[512,1024]{1,0:T(8,128)(2,1)} %param.10) | copy-start | bytes 3145732
  219.7 20.8 %collective-permute-start.5 = (bf16[512,256]{1,0:T(8,128)(2,1)S(1)}, bf16[512,256]{1,0:T(8,128)(2,1)S(1)}, u32[]{:S(2)}, u32[]{:S(2)}) collective-permute-start(bf16[512,256]{1,0:T(8,128)(2,1)S(1)} %convert_element_type.21), channel_id=1, source_target_pairs={{0,0},{1,8},{2,16},{3,24},{4,1},{5,9},{6,17},{7,25},{8,2},{9,10},{... | collective-permute-start | bytes 786440 | tf_op jit(solution)/shard_map/ppermute | solution.py:104
Sparse Core Ops, SparseCore 0:
  29.4 32.7 all-gather.1
  85.8 37.1 reduce-scatter.4
  163.7 54.7 reduce-scatter.2
